TPU v7x, 512 devices: a whole 4x8x8 slice. The times are simulated.
512 devices in a mesh: section: 32 (over z, x), neuron: 16 (over y, core).
Axes of the slice: x: 4, y: 8, z: 8, core: 2. Of those that a mesh axis runs over, the one named last changes fastest.
Arguments:
- inputs: bfloat16 [6, 32768], P(None, 'neuron'), may hold values from 0 to 2
- weight_tiles: bfloat16 [32, 2048, 128, 128], P('section', 'neuron'), may hold values from -0.07324219 to 0.07910156
- source_block: int32 [32, 2048], P('section', 'neuron'), may hold values from 0 to 255
- target_block: int32 [32, 2048], P('section', 'neuron'), may hold values from 0 to 15
- live_slots: int32 [32, 16], P('section', 'neuron'), may hold values from 16 to 128, as said below
Outputs:
- activations: bfloat16 [32, 6, 32768], P('section', None, 'neuron')
Inputs may be any that keep to these rules, and one draw needn't show every extreme that they name: live_slots[l, n] is 128, 64, 32 or 16, and in every layer some shard has all 128 slots live.
All inputs are finite; a program needn't handle non-finite values.
Results may differ from a plain program's by a relative error of at most 0.0045.
Values may be sent and summed in bfloat16 or wider, within the bound.
No kernel may reach another device: no remote copies, remote signals or barrier semaphores. Data moves between devices by JAX's collectives and lax.ppermute only.
A program may use at most 64 MiB of HBM per device.

v0:
```python
import jax
import jax.numpy as jnp
from jax import lax
from jax.sharding import PartitionSpec as P

MB = 3
NEURON_BIAS = -0.3
CLIP_LEVEL = 32.0


def from_behind(block, axis, distance):
    devices = range(lax.axis_size(axis))
    route = [(i - distance, i) for i in devices if i - distance in devices]
    return lax.ppermute(block, axis, route)


def layer_apply(gathered, weight_tiles, source_block, target_block, live_slots, column_count):
    row_count = gathered.shape[0]
    slot_count = weight_tiles.shape[1]
    block_size = weight_tiles.shape[2]
    block_count = gathered.shape[1] // block_size
    shaped = gathered.reshape(row_count, block_count, block_size)
    picked = jnp.take(shaped, source_block[0], axis=1)
    partial_value = jnp.einsum(
        "msk,skj->msj", picked, weight_tiles[0], preferred_element_type=jnp.float32
    )
    live_mask = jnp.arange(slot_count, dtype=jnp.int32) < live_slots[0, 0]
    selector = (
        target_block[0][:, None] == jnp.arange(column_count, dtype=jnp.int32)[None, :]
    ) & live_mask[:, None]
    summed = jnp.einsum(
        "msj,sc->mcj", partial_value, selector.astype(jnp.float32), precision=lax.Precision.HIGHEST
    )
    result = jnp.clip(summed + NEURON_BIAS, 0.0, CLIP_LEVEL).astype(jnp.bfloat16)
    return result.reshape(row_count, column_count * block_size)


def local(inputs, weight_tiles, source_block, target_block, live_slots):
    section_pos = lax.axis_index("section")
    section_count = lax.axis_size("section")
    total_rows = inputs.shape[0]
    shard_width = inputs.shape[1]
    column_count = shard_width // weight_tiles.shape[2]
    group_count = MB
    group_rows = total_rows // group_count
    step_count = section_count + group_count - 1

    def compute_layer(gathered):
        return layer_apply(
            gathered, weight_tiles, source_block, target_block, live_slots, column_count
        )

    def empty_layer(gathered):
        return jnp.zeros((group_rows, shard_width), jnp.bfloat16)

    def store_rows(collected, result, micro_index, active):
        row_start = jnp.clip(micro_index, 0, group_count - 1) * group_rows
        previous = lax.dynamic_slice_in_dim(collected, row_start, group_rows, 0)
        return lax.dynamic_update_slice_in_dim(
            collected, jnp.where(active, result, previous), row_start, 0
        )

    def input_rows(source, step_num):
        row_start = jnp.clip(step_num, 0, group_count - 1) * group_rows
        return lax.dynamic_slice_in_dim(source, row_start, group_rows, 0)

    collected = jnp.zeros((total_rows, shard_width), jnp.bfloat16)

    def advance(step_num, state_pair):
        current_in, collected = state_pair
        micro_index = step_num - section_pos
        active = (micro_index >= 0) & (micro_index < group_count)
        gathered = lax.all_gather(current_in, "neuron", axis=1, tiled=True)
        result = lax.cond(active, compute_layer, empty_layer, gathered)
        collected = store_rows(collected, result, micro_index, active)
        shifted = from_behind(result, "section", 1)
        current_in = jnp.where(section_pos == 0, input_rows(inputs, step_num + 1), shifted)
        return (current_in, collected)

    initial = input_rows(inputs, 0)
    final_in, collected = lax.fori_loop(0, step_count, advance, (initial, collected))
    return collected[None]


def solution(mesh):
    in_specs = (
        P(None, "neuron"),
        P("section", "neuron", None, None),
        P("section", "neuron"),
        P("section", "neuron"),
        P("section", "neuron"),
    )
    out_specs = P("section", None, "neuron")
    return jax.shard_map(local, mesh=mesh, in_specs=in_specs, out_specs=out_specs, check_vma=False)
```

profile of v0, /device:TPU:454, one launch (start us, length us, event | category | flops | bytes accessed | tf_op | source)
XLA Modules:
  0.0 940.5 jit_solution(12196027385270208893)
XLA Ops:
  0.8 939.1 %while.16 = (s32[]{:T(128)}, bf16[2,2048]{1,0:T(2,128)(2,1)S(1)}, bf16[6,2048]{1,0:T(8,128)(2,1)S(1)}, pred[]{:T(512)}, bf16[6,2048]{1,0:T(8,128)(2,1)}, /*index...) while((s32[]{:T(128)}, bf16[2,2048]{1,0:T(2,128)(2,1)S(1)}, ...), condition=%wide.region_3.0_spmd, body=%wide.region_0.3_spmd.sunk | while | flops 14739731 | bytes 4908993 | solution.py:81
  0.8 17.9 %all_gather.9 = bf16[2,32768]{1,0:T(2,128)(2,1)S(1)} all-gather(bf16[2,2048]{1,0:T(2,128)(2,1)S(1)} %get-tuple-element.321), channel_id=1, replica_groups=mesh['section'=32,'neuron'=16] {'neuron'}, dimensions={1}, use_global_device_ids=true | all-gather | bytes 139264 | tf_op jit(solution)/shard_map/while/body/eval_jaxpr/all_gather | solution.py:73
  25.1 15.3 %all_gather.9 = bf16[2,32768]{1,0:T(2,128)(2,1)S(1)} all-gather(bf16[2,2048]{1,0:T(2,128)(2,1)S(1)} %get-tuple-element.321), channel_id=1, replica_groups=mesh['section'=32,'neuron'=16] {'neuron'}, dimensions={1}, use_global_device_ids=true | all-gather | bytes 139264 | tf_op jit(solution)/shard_map/while/body/eval_jaxpr/all_gather | solution.py:73
  46.7 15.7 %all_gather.9 = bf16[2,32768]{1,0:T(2,128)(2,1)S(1)} all-gather(bf16[2,2048]{1,0:T(2,128)(2,1)S(1)} %get-tuple-element.321), channel_id=1, replica_groups=mesh['section'=32,'neuron'=16] {'neuron'}, dimensions={1}, use_global_device_ids=true | all-gather | bytes 139264 | tf_op jit(solution)/shard_map/while/body/eval_jaxpr/all_gather | solution.py:73
  68.7 15.3 %all_gather.9 = bf16[2,32768]{1,0:T(2,128)(2,1)S(1)} all-gather(bf16[2,2048]{1,0:T(2,128)(2,1)S(1)} %get-tuple-element.321), channel_id=1, replica_groups=mesh['section'=32,'neuron'=16] {'neuron'}, dimensions={1}, use_global_device_ids=true | all-gather | bytes 139264 | tf_op jit(solution)/shard_map/while/body/eval_jaxpr/all_gather | solution.py:73
  90.4 15.7 %all_gather.9 = bf16[2,32768]{1,0:T(2,128)(2,1)S(1)} all-gather(bf16[2,2048]{1,0:T(2,128)(2,1)S(1)} %get-tuple-element.321), channel_id=1, replica_groups=mesh['section'=32,'neuron'=16] {'neuron'}, dimensions={1}, use_global_device_ids=true | all-gather | bytes 139264 | tf_op jit(solution)/shard_map/while/body/eval_jaxpr/all_gather | solution.py:73
  112.5 15.3 %all_gather.9 = bf16[2,32768]{1,0:T(2,128)(2,1)S(1)} all-gather(bf16[2,2048]{1,0:T(2,128)(2,1)S(1)} %get-tuple-element.321), channel_id=1, replica_groups=mesh['section'=32,'neuron'=16] {'neuron'}, dimensions={1}, use_global_device_ids=true | all-gather | bytes 139264 | tf_op jit(solution)/shard_map/while/body/eval_jaxpr/all_gather | solution.py:73
  129.1 6.3 collective-permute-done
  136.2 15.7 %all_gather.9 = bf16[2,32768]{1,0:T(2,128)(2,1)S(1)} all-gather(bf16[2,2048]{1,0:T(2,128)(2,1)S(1)} %get-tuple-element.321), channel_id=1, replica_groups=mesh['section'=32,'neuron'=16] {'neuron'}, dimensions={1}, use_global_device_ids=true | all-gather | bytes 139264 | tf_op jit(solution)/shard_map/while/body/eval_jaxpr/all_gather | solution.py:73
  153.3 6.3 collective-permute-done
  160.4 15.3 %all_gather.9 = bf16[2,32768]{1,0:T(2,128)(2,1)S(1)} all-gather(bf16[2,2048]{1,0:T(2,128)(2,1)S(1)} %get-tuple-element.321), channel_id=1, replica_groups=mesh['section'=32,'neuron'=16] {'neuron'}, dimensions={1}, use_global_device_ids=true | all-gather | bytes 139264 | tf_op jit(solution)/shard_map/while/body/eval_jaxpr/all_gather | solution.py:73
  177.0 6.3 collective-permute-done
  184.1 15.7 %all_gather.9 = bf16[2,32768]{1,0:T(2,128)(2,1)S(1)} all-gather(bf16[2,2048]{1,0:T(2,128)(2,1)S(1)} %get-tuple-element.321), channel_id=1, replica_groups=mesh['section'=32,'neuron'=16] {'neuron'}, dimensions={1}, use_global_device_ids=true | all-gather | bytes 139264 | tf_op jit(solution)/shard_map/while/body/eval_jaxpr/all_gather | solution.py:73
  201.1 6.3 collective-permute-done
  208.2 15.3 %all_gather.9 = bf16[2,32768]{1,0:T(2,128)(2,1)S(1)} all-gather(bf16[2,2048]{1,0:T(2,128)(2,1)S(1)} %get-tuple-element.321), channel_id=1, replica_groups=mesh['section'=32,'neuron'=16] {'neuron'}, dimensions={1}, use_global_device_ids=true | all-gather | bytes 139264 | tf_op jit(solution)/shard_map/while/body/eval_jaxpr/all_gather | solution.py:73
  224.9 6.3 collective-permute-done
  232.0 15.7 %all_gather.9 = bf16[2,32768]{1,0:T(2,128)(2,1)S(1)} all-gather(bf16[2,2048]{1,0:T(2,128)(2,1)S(1)} %get-tuple-element.321), channel_id=1, replica_groups=mesh['section'=32,'neuron'=16] {'neuron'}, dimensions={1}, use_global_device_ids=true | all-gather | bytes 139264 | tf_op jit(solution)/shard_map/while/body/eval_jaxpr/all_gather | solution.py:73
  249.0 6.3 collective-permute-done
  256.1 15.3 %all_gather.9 = bf16[2,32768]{1,0:T(2,128)(2,1)S(1)} all-gather(bf16[2,2048]{1,0:T(2,128)(2,1)S(1)} %get-tuple-element.321), channel_id=1, replica_groups=mesh['section'=32,'neuron'=16] {'neuron'}, dimensions={1}, use_global_device_ids=true | all-gather | bytes 139264 | tf_op jit(solution)/shard_map/while/body/eval_jaxpr/all_gather | solution.py:73
  272.8 6.3 collective-permute-done
  279.9 15.7 %all_gather.9 = bf16[2,32768]{1,0:T(2,128)(2,1)S(1)} all-gather(bf16[2,2048]{1,0:T(2,128)(2,1)S(1)} %get-tuple-element.321), channel_id=1, replica_groups=mesh['section'=32,'neuron'=16] {'neuron'}, dimensions={1}, use_global_device_ids=true | all-gather | bytes 139264 | tf_op jit(solution)/shard_map/while/body/eval_jaxpr/all_gather | solution.py:73
  296.9 6.3 collective-permute-done
  304.0 15.3 %all_gather.9 = bf16[2,32768]{1,0:T(2,128)(2,1)S(1)} all-gather(bf16[2,2048]{1,0:T(2,128)(2,1)S(1)} %get-tuple-element.321), channel_id=1, replica_groups=mesh['section'=32,'neuron'=16] {'neuron'}, dimensions={1}, use_global_device_ids=true | all-gather | bytes 139264 | tf_op jit(solution)/shard_map/while/body/eval_jaxpr/all_gather | solution.py:73
  320.6 6.3 collective-permute-done
  327.7 15.7 %all_gather.9 = bf16[2,32768]{1,0:T(2,128)(2,1)S(1)} all-gather(bf16[2,2048]{1,0:T(2,128)(2,1)S(1)} %get-tuple-element.321), channel_id=1, replica_groups=mesh['section'=32,'neuron'=16] {'neuron'}, dimensions={1}, use_global_device_ids=true | all-gather | bytes 139264 | tf_op jit(solution)/shard_map/while/body/eval_jaxpr/all_gather | solution.py:73
  344.8 6.3 collective-permute-done
  351.9 15.3 %all_gather.9 = bf16[2,32768]{1,0:T(2,128)(2,1)S(1)} all-gather(bf16[2,2048]{1,0:T(2,128)(2,1)S(1)} %get-tuple-element.321), channel_id=1, replica_groups=mesh['section'=32,'neuron'=16] {'neuron'}, dimensions={1}, use_global_device_ids=true | all-gather | bytes 139264 | tf_op jit(solution)/shard_map/while/body/eval_jaxpr/all_gather | solution.py:73
  368.5 6.3 collective-permute-done
  375.6 15.7 %all_gather.9 = bf16[2,32768]{1,0:T(2,128)(2,1)S(1)} all-gather(bf16[2,2048]{1,0:T(2,128)(2,1)S(1)} %get-tuple-element.321), channel_id=1, replica_groups=mesh['section'=32,'neuron'=16] {'neuron'}, dimensions={1}, use_global_device_ids=true | all-gather | bytes 139264 | tf_op jit(solution)/shard_map/while/body/eval_jaxpr/all_gather | solution.py:73
  392.7 6.3 collective-permute-done
  399.8 15.3 %all_gather.9 = bf16[2,32768]{1,0:T(2,128)(2,1)S(1)} all-gather(bf16[2,2048]{1,0:T(2,128)(2,1)S(1)} %get-tuple-element.321), channel_id=1, replica_groups=mesh['section'=32,'neuron'=16] {'neuron'}, dimensions={1}, use_global_device_ids=true | all-gather | bytes 139264 | tf_op jit(solution)/shard_map/while/body/eval_jaxpr/all_gather | solution.py:73
  416.4 6.3 collective-permute-done
  423.5 15.7 %all_gather.9 = bf16[2,32768]{1,0:T(2,128)(2,1)S(1)} all-gather(bf16[2,2048]{1,0:T(2,128)(2,1)S(1)} %get-tuple-element.321), channel_id=1, replica_groups=mesh['section'=32,'neuron'=16] {'neuron'}, dimensions={1}, use_global_device_ids=true | all-gather | bytes 139264 | tf_op jit(solution)/shard_map/while/body/eval_jaxpr/all_gather | solution.py:73
  440.5 6.3 collective-permute-done
  447.6 15.3 %all_gather.9 = bf16[2,32768]{1,0:T(2,128)(2,1)S(1)} all-gather(bf16[2,2048]{1,0:T(2,128)(2,1)S(1)} %get-tuple-element.321), channel_id=1, replica_groups=mesh['section'=32,'neuron'=16] {'neuron'}, dimensions={1}, use_global_device_ids=true | all-gather | bytes 139264 | tf_op jit(solution)/shard_map/while/body/eval_jaxpr/all_gather | solution.py:73
  464.3 6.3 collective-permute-done
  471.4 15.7 %all_gather.9 = bf16[2,32768]{1,0:T(2,128)(2,1)S(1)} all-gather(bf16[2,2048]{1,0:T(2,128)(2,1)S(1)} %get-tuple-element.321), channel_id=1, replica_groups=mesh['section'=32,'neuron'=16] {'neuron'}, dimensions={1}, use_global_device_ids=true | all-gather | bytes 139264 | tf_op jit(solution)/shard_map/while/body/eval_jaxpr/all_gather | solution.py:73
  488.4 6.3 collective-permute-done
  495.5 15.3 %all_gather.9 = bf16[2,32768]{1,0:T(2,128)(2,1)S(1)} all-gather(bf16[2,2048]{1,0:T(2,128)(2,1)S(1)} %get-tuple-element.321), channel_id=1, replica_groups=mesh['section'=32,'neuron'=16] {'neuron'}, dimensions={1}, use_global_device_ids=true | all-gather | bytes 139264 | tf_op jit(solution)/shard_map/while/body/eval_jaxpr/all_gather | solution.py:73
  512.2 6.3 collective-permute-done
  519.3 15.7 %all_gather.9 = bf16[2,32768]{1,0:T(2,128)(2,1)S(1)} all-gather(bf16[2,2048]{1,0:T(2,128)(2,1)S(1)} %get-tuple-element.321), channel_id=1, replica_groups=mesh['section'=32,'neuron'=16] {'neuron'}, dimensions={1}, use_global_device_ids=true | all-gather | bytes 139264 | tf_op jit(solution)/shard_map/while/body/eval_jaxpr/all_gather | solution.py:73
  536.3 6.3 collective-permute-done
  543.4 15.3 %all_gather.9 = bf16[2,32768]{1,0:T(2,128)(2,1)S(1)} all-gather(bf16[2,2048]{1,0:T(2,128)(2,1)S(1)} %get-tuple-element.321), channel_id=1, replica_groups=mesh['section'=32,'neuron'=16] {'neuron'}, dimensions={1}, use_global_device_ids=true | all-gather | bytes 139264 | tf_op jit(solution)/shard_map/while/body/eval_jaxpr/all_gather | solution.py:73
  560.0 6.3 collective-permute-done
  567.1 15.7 %all_gather.9 = bf16[2,32768]{1,0:T(2,128)(2,1)S(1)} all-gather(bf16[2,2048]{1,0:T(2,128)(2,1)S(1)} %get-tuple-element.321), channel_id=1, replica_groups=mesh['section'=32,'neuron'=16] {'neuron'}, dimensions={1}, use_global_device_ids=true | all-gather | bytes 139264 | tf_op jit(solution)/shard_map/while/body/eval_jaxpr/all_gather | solution.py:73
  584.2 6.3 collective-permute-done
  591.3 15.3 %all_gather.9 = bf16[2,32768]{1,0:T(2,128)(2,1)S(1)} all-gather(bf16[2,2048]{1,0:T(2,128)(2,1)S(1)} %get-tuple-element.321), channel_id=1, replica_groups=mesh['section'=32,'neuron'=16] {'neuron'}, dimensions={1}, use_global_device_ids=true | all-gather | bytes 139264 | tf_op jit(solution)/shard_map/while/body/eval_jaxpr/all_gather | solution.py:73
  607.9 6.3 collective-permute-done
  615.0 15.7 %all_gather.9 = bf16[2,32768]{1,0:T(2,128)(2,1)S(1)} all-gather(bf16[2,2048]{1,0:T(2,128)(2,1)S(1)} %get-tuple-element.321), channel_id=1, replica_groups=mesh['section'=32,'neuron'=16] {'neuron'}, dimensions={1}, use_global_device_ids=true | all-gather | bytes 139264 | tf_op jit(solution)/shard_map/while/body/eval_jaxpr/all_gather | solution.py:73
  632.1 6.3 collective-permute-done
  639.2 15.3 %all_gather.9 = bf16[2,32768]{1,0:T(2,128)(2,1)S(1)} all-gather(bf16[2,2048]{1,0:T(2,128)(2,1)S(1)} %get-tuple-element.321), channel_id=1, replica_groups=mesh['section'=32,'neuron'=16] {'neuron'}, dimensions={1}, use_global_device_ids=true | all-gather | bytes 139264 | tf_op jit(solution)/shard_map/while/body/eval_jaxpr/all_gather | solution.py:73
  662.9 15.7 %all_gather.9 = bf16[2,32768]{1,0:T(2,128)(2,1)S(1)} all-gather(bf16[2,2048]{1,0:T(2,128)(2,1)S(1)} %get-tuple-element.321), channel_id=1, replica_groups=mesh['section'=32,'neuron'=16] {'neuron'}, dimensions={1}, use_global_device_ids=true | all-gather | bytes 139264 | tf_op jit(solution)/shard_map/while/body/eval_jaxpr/all_gather | solution.py:73
  687.0 15.3 %all_gather.9 = bf16[2,32768]{1,0:T(2,128)(2,1)S(1)} all-gather(bf16[2,2048]{1,0:T(2,128)(2,1)S(1)} %get-tuple-element.321), channel_id=1, replica_groups=mesh['section'=32,'neuron'=16] {'neuron'}, dimensions={1}, use_global_device_ids=true | all-gather | bytes 139264 | tf_op jit(solution)/shard_map/while/body/eval_jaxpr/all_gather | solution.py:73
  703.7 6.3 collective-permute-done
  710.8 15.7 %all_gather.9 = bf16[2,32768]{1,0:T(2,128)(2,1)S(1)} all-gather(bf16[2,2048]{1,0:T(2,128)(2,1)S(1)} %get-tuple-element.321), channel_id=1, replica_groups=mesh['section'=32,'neuron'=16] {'neuron'}, dimensions={1}, use_global_device_ids=true | all-gather | bytes 139264 | tf_op jit(solution)/shard_map/while/body/eval_jaxpr/all_gather | solution.py:73
  727.8 119.0 %collective-permute-done = bf16[2,2048]{1,0:T(2,128)(2,1)S(1)} collective-permute-done((bf16[2,2048]{1,0:T(2,128)(2,1)S(1)}, bf16[2,2048]{1,0:T(2,128)(2,1)S(1)}, u32[]{:S(2)}, u32[]{:S(2)}) %collective-permute-start) | collective-permute-done | bytes 8224 | tf_op jit(solution)/shard_map/while/body/eval_jaxpr/ppermute | solution.py:14
  847.6 16.5 %all_gather.9 = bf16[2,32768]{1,0:T(2,128)(2,1)S(1)} all-gather(bf16[2,2048]{1,0:T(2,128)(2,1)S(1)} %get-tuple-element.321), channel_id=1, replica_groups=mesh['section'=32,'neuron'=16] {'neuron'}, dimensions={1}, use_global_device_ids=true | all-gather | bytes 139264 | tf_op jit(solution)/shard_map/while/body/eval_jaxpr/all_gather | solution.py:73
  864.1 6.4 conditional.2
  871.8 7.5 collective-permute-done
  880.1 14.5 %all_gather.9 = bf16[2,32768]{1,0:T(2,128)(2,1)S(1)} all-gather(bf16[2,2048]{1,0:T(2,128)(2,1)S(1)} %get-tuple-element.321), channel_id=1, replica_groups=mesh['section'=32,'neuron'=16] {'neuron'}, dimensions={1}, use_global_device_ids=true | all-gather | bytes 139264 | tf_op jit(solution)/shard_map/while/body/eval_jaxpr/all_gather | solution.py:73
  894.7 6.4 conditional.2
  902.4 7.5 collective-permute-done
  910.7 16.5 %all_gather.9 = bf16[2,32768]{1,0:T(2,128)(2,1)S(1)} all-gather(bf16[2,2048]{1,0:T(2,128)(2,1)S(1)} %get-tuple-element.321), channel_id=1, replica_groups=mesh['section'=32,'neuron'=16] {'neuron'}, dimensions={1}, use_global_device_ids=true | all-gather | bytes 139264 | tf_op jit(solution)/shard_map/while/body/eval_jaxpr/all_gather | solution.py:73
  927.2 6.4 conditional.2
  (206 shorter events, 129.7 us)
Async XLA Ops:
  18.7 5.5 collective-permute-start
  40.4 5.5 collective-permute-start
  62.4 5.5 collective-permute-start
  84.0 5.5 collective-permute-start
  106.1 5.6 collective-permute-start
  127.8 7.6 collective-permute-start
  151.9 7.6 collective-permute-start
  175.6 7.6 collective-permute-start
  199.8 7.6 collective-permute-start
  223.5 7.6 collective-permute-start
  247.7 7.6 collective-permute-start
  271.4 7.6 collective-permute-start
  295.5 7.6 collective-permute-start
  319.3 7.6 collective-permute-start
  343.4 7.6 collective-permute-start
  367.2 7.6 collective-permute-start
  391.3 7.6 collective-permute-start
  415.0 7.6 collective-permute-start
  439.2 7.6 collective-permute-start
  462.9 7.6 collective-permute-start
  487.1 7.6 collective-permute-start
  510.8 7.6 collective-permute-start
  534.9 7.6 collective-permute-start
  558.7 7.6 collective-permute-start
  582.8 7.6 collective-permute-start
  606.6 7.6 collective-permute-start
  630.7 7.6 collective-permute-start
  654.4 7.6 collective-permute-start
  678.6 7.6 collective-permute-start
  702.3 7.6 collective-permute-start
  726.5 120.4 %collective-permute-start = (bf16[2,2048]{1,0:T(2,128)(2,1)S(1)}, bf16[2,2048]{1,0:T(2,128)(2,1)S(1)}, u32[]{:S(2)}, u32[]{:S(2)}) collective-permute-start(bf16[2,2048]{1,0:T(2,128)(2,1)S(1)} %get-tuple-element.350), channel_id=1, source_target_pairs={{0,16},{16,32},{32,48},{48,64},{64,80},{80,96},{96,112},{112,128},... | collective-permute-start | bytes 24584 | tf_op jit(solution)/shard_map/while/body/eval_jaxpr/ppermute | solution.py:14
  864.1 6.2 copy-start.1
  870.5 8.9 collective-permute-start
  894.7 6.2 copy-start.1
  901.0 8.9 collective-permute-start
  927.2 6.2 copy-start.1
  933.5 5.5 collective-permute-start
  939.9 0.6 copy-start
where the time goes:
time: 944 us; the launch traced here: 940 us
  blocking collectives  530 us (56%)
  waiting for transfers between devices  317 us (34%)
  starting transfers between devices  43.6 us (5%)
  other arithmetic  33.6 us (4%)
  matrix products  10.8 us (1%)
    all_gather x34, blocking collectives, advance(): gathered = lax.all_gather(current_in, 'neuron', axis=1, tiled=True)  530 us
    ppermute x34, waiting for transfers between devices, from_behind(): return lax.ppermute(block, axis, route)  317 us
    ppermute x34, starting transfers between devices, from_behind(): return lax.ppermute(block, axis, route)  43.6 us
    select_n x34, other arithmetic, advance(): jnp.where(section_pos == 0, input_rows(inputs, step_num + 1), shifted)  26.4 us
  transfers between devices with their start and end apart: 34, of which 34 were waited for; matrix products, arithmetic and copies ran while one was open for 0% of the time, Pallas kernels for 0%

commit v1 on v0

--- a/solution.py
+++ b/solution.py
@@ -70,7 +70,10 @@
         current_in, collected = state_pair
         micro_index = step_num - section_pos
         active = (micro_index >= 0) & (micro_index < group_count)
-        gathered = lax.all_gather(current_in, "neuron", axis=1, tiled=True)
+        gathered = jnp.concatenate(
+            lax.all_to_all(jnp.stack([current_in] * lax.axis_size("neuron")), "neuron", 0, 0),
+            axis=1,
+        )
         result = lax.cond(active, compute_layer, empty_layer, gathered)
         collected = store_rows(collected, result, micro_index, active)
         shifted = from_behind(result, "section", 1)

time: 944 us -> 857 us (0.908)
  blocking collectives: 530 us -> 0 us
  waiting for transfers between devices: 317 us -> 609 us
  starting transfers between devices: 43.6 us -> 167 us
  local copies, waits for them, and re-layouts: 3.82 us -> 28.4 us
    all_gather x34 -> x0, blocking collectives: 530 us -> none  [advance(): gathered = lax.all_gather(current_in, 'neuron', axis=1, tiled=True)]
    all_to_all x0 -> x34, waiting for transfers between devices: none -> 292 us  [advance(): lax.all_to_all(jnp.stack([current_in] * lax.axis_size('neuron')), 'neuron...]
    all_to_all x0 -> x34, starting transfers between devices: none -> 123 us  [advance(): lax.all_to_all(jnp.stack([current_in] * lax.axis_size('neuron')), 'neuron...]
    another operation x31 -> x65, local copies, waits for them, and re-layouts: 0.21 us -> 24.8 us  [the longest x34 24.6 us: advance(): jnp.stack([current_in] * lax.axis_size('neuron'))]
  transfers between devices with their start and end apart: 34 -> 68, of which waited for: 34 -> 68; matrix products, arithmetic and copies ran while one was open for 0% -> 0% of each run, Pallas kernels for 0% -> 0%
where the time goes in v1:
time: 857 us; the launch traced here: 851 us
  waiting for transfers between devices  609 us (71%)
  starting transfers between devices  167 us (19%)
  other arithmetic  33.6 us (4%)
  local copies, waits for them, and re-layouts  28.4 us (3%)
  matrix products  10.8 us (1%)
    ppermute x34, waiting for transfers between devices, from_behind(): return lax.ppermute(block, axis, route)  317 us
    all_to_all x34, waiting for transfers between devices, advance(): lax.all_to_all(jnp.stack([current_in] * lax.axis_size('neuron')), 'neuron...  292 us
    all_to_all x34, starting transfers between devices, advance(): lax.all_to_all(jnp.stack([current_in] * lax.axis_size('neuron')), 'neuron...  123 us
    ppermute x34, starting transfers between devices, from_behind(): return lax.ppermute(block, axis, route)  43.9 us
    select_n x34, other arithmetic, advance(): jnp.where(section_pos == 0, input_rows(inputs, step_num + 1), shifted)  26.4 us
    another operation x34, local copies, waits for them, and re-layouts, advance(): jnp.stack([current_in] * lax.axis_size('neuron'))  24.6 us
  transfers between devices with their start and end apart: 68, of which 68 were waited for; matrix products, arithmetic and copies ran while one was open for 0% of the time, Pallas kernels for 0%

profile of v1, /device:TPU:454, one launch (start us, length us, event | category | flops | bytes accessed | tf_op | source)
XLA Modules:
  0.0 850.9 jit_solution(687123559328291019)
XLA Ops:
  0.8 849.5 %while.16 = (s32[]{:T(128)}, bf16[2,2048]{1,0:T(2,128)(2,1)S(1)}, bf16[6,2048]{1,0:T(8,128)(2,1)S(1)}, pred[]{:T(512)}, bf16[6,2048]{1,0:T(8,128)(2,1)}, /*index...) while((s32[]{:T(128)}, bf16[2,2048]{1,0:T(2,128)(2,1)S(1)}, ...), condition=%wide.region_3.0_spmd, body=%wide.region_0.3_spmd.sunk | while | flops 14739731 | bytes 5302241 | solution.py:84
  1.5 7.2 all-to-all-start
  8.8 8.6 %all-to-all-done = bf16[16,2,2048]{2,1,0:T(2,128)(2,1)S(1)} async-done(((bf16[16,2,2048]{2,1,0:T(2,128)(2,1)}), bf16[16,2,2048]{2,1,0:T(2,128)(2,1)S(1)}, u32[]{:S(2)}, u32[]{:S(2)}) %all-to-all-start) | async-done | bytes 131104 | tf_op jit(solution)/shard_map/while/body/eval_jaxpr/all_to_all | solution.py:74
  28.0 8.6 %all-to-all-done = bf16[16,2,2048]{2,1,0:T(2,128)(2,1)S(1)} async-done(((bf16[16,2,2048]{2,1,0:T(2,128)(2,1)}), bf16[16,2,2048]{2,1,0:T(2,128)(2,1)S(1)}, u32[]{:S(2)}, u32[]{:S(2)}) %all-to-all-start) | async-done | bytes 131104 | tf_op jit(solution)/shard_map/while/body/eval_jaxpr/all_to_all | solution.py:74
  47.2 8.6 %all-to-all-done = bf16[16,2,2048]{2,1,0:T(2,128)(2,1)S(1)} async-done(((bf16[16,2,2048]{2,1,0:T(2,128)(2,1)}), bf16[16,2,2048]{2,1,0:T(2,128)(2,1)S(1)}, u32[]{:S(2)}, u32[]{:S(2)}) %all-to-all-start) | async-done | bytes 131104 | tf_op jit(solution)/shard_map/while/body/eval_jaxpr/all_to_all | solution.py:74
  66.4 8.6 %all-to-all-done = bf16[16,2,2048]{2,1,0:T(2,128)(2,1)S(1)} async-done(((bf16[16,2,2048]{2,1,0:T(2,128)(2,1)}), bf16[16,2,2048]{2,1,0:T(2,128)(2,1)S(1)}, u32[]{:S(2)}, u32[]{:S(2)}) %all-to-all-start) | async-done | bytes 131104 | tf_op jit(solution)/shard_map/while/body/eval_jaxpr/all_to_all | solution.py:74
  85.6 8.6 %all-to-all-done = bf16[16,2,2048]{2,1,0:T(2,128)(2,1)S(1)} async-done(((bf16[16,2,2048]{2,1,0:T(2,128)(2,1)}), bf16[16,2,2048]{2,1,0:T(2,128)(2,1)S(1)}, u32[]{:S(2)}, u32[]{:S(2)}) %all-to-all-start) | async-done | bytes 131104 | tf_op jit(solution)/shard_map/while/body/eval_jaxpr/all_to_all | solution.py:74
  104.9 8.6 %all-to-all-done = bf16[16,2,2048]{2,1,0:T(2,128)(2,1)S(1)} async-done(((bf16[16,2,2048]{2,1,0:T(2,128)(2,1)}), bf16[16,2,2048]{2,1,0:T(2,128)(2,1)S(1)}, u32[]{:S(2)}, u32[]{:S(2)}) %all-to-all-start) | async-done | bytes 131104 | tf_op jit(solution)/shard_map/while/body/eval_jaxpr/all_to_all | solution.py:74
  114.8 6.3 collective-permute-done
  126.2 8.6 %all-to-all-done = bf16[16,2,2048]{2,1,0:T(2,128)(2,1)S(1)} async-done(((bf16[16,2,2048]{2,1,0:T(2,128)(2,1)}), bf16[16,2,2048]{2,1,0:T(2,128)(2,1)S(1)}, u32[]{:S(2)}, u32[]{:S(2)}) %all-to-all-start) | async-done | bytes 131104 | tf_op jit(solution)/shard_map/while/body/eval_jaxpr/all_to_all | solution.py:74
  136.2 6.3 collective-permute-done
  147.5 8.6 %all-to-all-done = bf16[16,2,2048]{2,1,0:T(2,128)(2,1)S(1)} async-done(((bf16[16,2,2048]{2,1,0:T(2,128)(2,1)}), bf16[16,2,2048]{2,1,0:T(2,128)(2,1)S(1)}, u32[]{:S(2)}, u32[]{:S(2)}) %all-to-all-start) | async-done | bytes 131104 | tf_op jit(solution)/shard_map/while/body/eval_jaxpr/all_to_all | solution.py:74
  157.5 6.3 collective-permute-done
  168.9 8.6 %all-to-all-done = bf16[16,2,2048]{2,1,0:T(2,128)(2,1)S(1)} async-done(((bf16[16,2,2048]{2,1,0:T(2,128)(2,1)}), bf16[16,2,2048]{2,1,0:T(2,128)(2,1)S(1)}, u32[]{:S(2)}, u32[]{:S(2)}) %all-to-all-start) | async-done | bytes 131104 | tf_op jit(solution)/shard_map/while/body/eval_jaxpr/all_to_all | solution.py:74
  178.8 6.3 collective-permute-done
  190.2 8.6 %all-to-all-done = bf16[16,2,2048]{2,1,0:T(2,128)(2,1)S(1)} async-done(((bf16[16,2,2048]{2,1,0:T(2,128)(2,1)}), bf16[16,2,2048]{2,1,0:T(2,128)(2,1)S(1)}, u32[]{:S(2)}, u32[]{:S(2)}) %all-to-all-start) | async-done | bytes 131104 | tf_op jit(solution)/shard_map/while/body/eval_jaxpr/all_to_all | solution.py:74
  200.1 6.3 collective-permute-done
  211.5 8.6 %all-to-all-done = bf16[16,2,2048]{2,1,0:T(2,128)(2,1)S(1)} async-done(((bf16[16,2,2048]{2,1,0:T(2,128)(2,1)}), bf16[16,2,2048]{2,1,0:T(2,128)(2,1)S(1)}, u32[]{:S(2)}, u32[]{:S(2)}) %all-to-all-start) | async-done | bytes 131104 | tf_op jit(solution)/shard_map/while/body/eval_jaxpr/all_to_all | solution.py:74
  221.4 6.3 collective-permute-done
  232.8 8.6 %all-to-all-done = bf16[16,2,2048]{2,1,0:T(2,128)(2,1)S(1)} async-done(((bf16[16,2,2048]{2,1,0:T(2,128)(2,1)}), bf16[16,2,2048]{2,1,0:T(2,128)(2,1)S(1)}, u32[]{:S(2)}, u32[]{:S(2)}) %all-to-all-start) | async-done | bytes 131104 | tf_op jit(solution)/shard_map/while/body/eval_jaxpr/all_to_all | solution.py:74
  242.8 6.3 collective-permute-done
  254.1 8.6 %all-to-all-done = bf16[16,2,2048]{2,1,0:T(2,128)(2,1)S(1)} async-done(((bf16[16,2,2048]{2,1,0:T(2,128)(2,1)}), bf16[16,2,2048]{2,1,0:T(2,128)(2,1)S(1)}, u32[]{:S(2)}, u32[]{:S(2)}) %all-to-all-start) | async-done | bytes 131104 | tf_op jit(solution)/shard_map/while/body/eval_jaxpr/all_to_all | solution.py:74
  264.1 6.3 collective-permute-done
  275.5 8.6 %all-to-all-done = bf16[16,2,2048]{2,1,0:T(2,128)(2,1)S(1)} async-done(((bf16[16,2,2048]{2,1,0:T(2,128)(2,1)}), bf16[16,2,2048]{2,1,0:T(2,128)(2,1)S(1)}, u32[]{:S(2)}, u32[]{:S(2)}) %all-to-all-start) | async-done | bytes 131104 | tf_op jit(solution)/shard_map/while/body/eval_jaxpr/all_to_all | solution.py:74
  285.4 6.3 collective-permute-done
  296.8 8.6 %all-to-all-done = bf16[16,2,2048]{2,1,0:T(2,128)(2,1)S(1)} async-done(((bf16[16,2,2048]{2,1,0:T(2,128)(2,1)}), bf16[16,2,2048]{2,1,0:T(2,128)(2,1)S(1)}, u32[]{:S(2)}, u32[]{:S(2)}) %all-to-all-start) | async-done | bytes 131104 | tf_op jit(solution)/shard_map/while/body/eval_jaxpr/all_to_all | solution.py:74
  306.7 6.3 collective-permute-done
  318.1 8.6 %all-to-all-done = bf16[16,2,2048]{2,1,0:T(2,128)(2,1)S(1)} async-done(((bf16[16,2,2048]{2,1,0:T(2,128)(2,1)}), bf16[16,2,2048]{2,1,0:T(2,128)(2,1)S(1)}, u32[]{:S(2)}, u32[]{:S(2)}) %all-to-all-start) | async-done | bytes 131104 | tf_op jit(solution)/shard_map/while/body/eval_jaxpr/all_to_all | solution.py:74
  328.0 6.3 collective-permute-done
  339.4 8.6 %all-to-all-done = bf16[16,2,2048]{2,1,0:T(2,128)(2,1)S(1)} async-done(((bf16[16,2,2048]{2,1,0:T(2,128)(2,1)}), bf16[16,2,2048]{2,1,0:T(2,128)(2,1)S(1)}, u32[]{:S(2)}, u32[]{:S(2)}) %all-to-all-start) | async-done | bytes 131104 | tf_op jit(solution)/shard_map/while/body/eval_jaxpr/all_to_all | solution.py:74
  349.3 6.3 collective-permute-done
  360.7 8.6 %all-to-all-done = bf16[16,2,2048]{2,1,0:T(2,128)(2,1)S(1)} async-done(((bf16[16,2,2048]{2,1,0:T(2,128)(2,1)}), bf16[16,2,2048]{2,1,0:T(2,128)(2,1)S(1)}, u32[]{:S(2)}, u32[]{:S(2)}) %all-to-all-start) | async-done | bytes 131104 | tf_op jit(solution)/shard_map/while/body/eval_jaxpr/all_to_all | solution.py:74
  370.7 6.3 collective-permute-done
  382.1 8.6 %all-to-all-done = bf16[16,2,2048]{2,1,0:T(2,128)(2,1)S(1)} async-done(((bf16[16,2,2048]{2,1,0:T(2,128)(2,1)}), bf16[16,2,2048]{2,1,0:T(2,128)(2,1)S(1)}, u32[]{:S(2)}, u32[]{:S(2)}) %all-to-all-start) | async-done | bytes 131104 | tf_op jit(solution)/shard_map/while/body/eval_jaxpr/all_to_all | solution.py:74
  392.0 6.3 collective-permute-done
  403.4 8.6 %all-to-all-done = bf16[16,2,2048]{2,1,0:T(2,128)(2,1)S(1)} async-done(((bf16[16,2,2048]{2,1,0:T(2,128)(2,1)}), bf16[16,2,2048]{2,1,0:T(2,128)(2,1)S(1)}, u32[]{:S(2)}, u32[]{:S(2)}) %all-to-all-start) | async-done | bytes 131104 | tf_op jit(solution)/shard_map/while/body/eval_jaxpr/all_to_all | solution.py:74
  424.7 8.6 %all-to-all-done = bf16[16,2,2048]{2,1,0:T(2,128)(2,1)S(1)} async-done(((bf16[16,2,2048]{2,1,0:T(2,128)(2,1)}), bf16[16,2,2048]{2,1,0:T(2,128)(2,1)S(1)}, u32[]{:S(2)}, u32[]{:S(2)}) %all-to-all-start) | async-done | bytes 131104 | tf_op jit(solution)/shard_map/while/body/eval_jaxpr/all_to_all | solution.py:74
  434.6 6.3 collective-permute-done
  446.0 8.6 %all-to-all-done = bf16[16,2,2048]{2,1,0:T(2,128)(2,1)S(1)} async-done(((bf16[16,2,2048]{2,1,0:T(2,128)(2,1)}), bf16[16,2,2048]{2,1,0:T(2,128)(2,1)S(1)}, u32[]{:S(2)}, u32[]{:S(2)}) %all-to-all-start) | async-done | bytes 131104 | tf_op jit(solution)/shard_map/while/body/eval_jaxpr/all_to_all | solution.py:74
  455.9 6.3 collective-permute-done
  467.3 8.6 %all-to-all-done = bf16[16,2,2048]{2,1,0:T(2,128)(2,1)S(1)} async-done(((bf16[16,2,2048]{2,1,0:T(2,128)(2,1)}), bf16[16,2,2048]{2,1,0:T(2,128)(2,1)S(1)}, u32[]{:S(2)}, u32[]{:S(2)}) %all-to-all-start) | async-done | bytes 131104 | tf_op jit(solution)/shard_map/while/body/eval_jaxpr/all_to_all | solution.py:74
  477.3 6.3 collective-permute-done
  488.6 8.6 %all-to-all-done = bf16[16,2,2048]{2,1,0:T(2,128)(2,1)S(1)} async-done(((bf16[16,2,2048]{2,1,0:T(2,128)(2,1)}), bf16[16,2,2048]{2,1,0:T(2,128)(2,1)S(1)}, u32[]{:S(2)}, u32[]{:S(2)}) %all-to-all-start) | async-done | bytes 131104 | tf_op jit(solution)/shard_map/while/body/eval_jaxpr/all_to_all | solution.py:74
  498.6 6.3 collective-permute-done
  510.0 8.6 %all-to-all-done = bf16[16,2,2048]{2,1,0:T(2,128)(2,1)S(1)} async-done(((bf16[16,2,2048]{2,1,0:T(2,128)(2,1)}), bf16[16,2,2048]{2,1,0:T(2,128)(2,1)S(1)}, u32[]{:S(2)}, u32[]{:S(2)}) %all-to-all-start) | async-done | bytes 131104 | tf_op jit(solution)/shard_map/while/body/eval_jaxpr/all_to_all | solution.py:74
  531.3 8.6 %all-to-all-done = bf16[16,2,2048]{2,1,0:T(2,128)(2,1)S(1)} async-done(((bf16[16,2,2048]{2,1,0:T(2,128)(2,1)}), bf16[16,2,2048]{2,1,0:T(2,128)(2,1)S(1)}, u32[]{:S(2)}, u32[]{:S(2)}) %all-to-all-start) | async-done | bytes 131104 | tf_op jit(solution)/shard_map/while/body/eval_jaxpr/all_to_all | solution.py:74
  541.2 6.3 collective-permute-done
  552.6 8.6 %all-to-all-done = bf16[16,2,2048]{2,1,0:T(2,128)(2,1)S(1)} async-done(((bf16[16,2,2048]{2,1,0:T(2,128)(2,1)}), bf16[16,2,2048]{2,1,0:T(2,128)(2,1)S(1)}, u32[]{:S(2)}, u32[]{:S(2)}) %all-to-all-start) | async-done | bytes 131104 | tf_op jit(solution)/shard_map/while/body/eval_jaxpr/all_to_all | solution.py:74
  562.5 6.3 collective-permute-done
  573.9 8.6 %all-to-all-done = bf16[16,2,2048]{2,1,0:T(2,128)(2,1)S(1)} async-done(((bf16[16,2,2048]{2,1,0:T(2,128)(2,1)}), bf16[16,2,2048]{2,1,0:T(2,128)(2,1)S(1)}, u32[]{:S(2)}, u32[]{:S(2)}) %all-to-all-start) | async-done | bytes 131104 | tf_op jit(solution)/shard_map/while/body/eval_jaxpr/all_to_all | solution.py:74
  595.2 8.6 %all-to-all-done = bf16[16,2,2048]{2,1,0:T(2,128)(2,1)S(1)} async-done(((bf16[16,2,2048]{2,1,0:T(2,128)(2,1)}), bf16[16,2,2048]{2,1,0:T(2,128)(2,1)S(1)}, u32[]{:S(2)}, u32[]{:S(2)}) %all-to-all-start) | async-done | bytes 131104 | tf_op jit(solution)/shard_map/while/body/eval_jaxpr/all_to_all | solution.py:74
  605.2 6.3 collective-permute-done
  616.6 8.6 %all-to-all-done = bf16[16,2,2048]{2,1,0:T(2,128)(2,1)S(1)} async-done(((bf16[16,2,2048]{2,1,0:T(2,128)(2,1)}), bf16[16,2,2048]{2,1,0:T(2,128)(2,1)S(1)}, u32[]{:S(2)}, u32[]{:S(2)}) %all-to-all-start) | async-done | bytes 131104 | tf_op jit(solution)/shard_map/while/body/eval_jaxpr/all_to_all | solution.py:74
  626.5 6.3 collective-permute-done
  637.9 8.6 %all-to-all-done = bf16[16,2,2048]{2,1,0:T(2,128)(2,1)S(1)} async-done(((bf16[16,2,2048]{2,1,0:T(2,128)(2,1)}), bf16[16,2,2048]{2,1,0:T(2,128)(2,1)S(1)}, u32[]{:S(2)}, u32[]{:S(2)}) %all-to-all-start) | async-done | bytes 131104 | tf_op jit(solution)/shard_map/while/body/eval_jaxpr/all_to_all | solution.py:74
  647.8 118.3 %collective-permute-done = bf16[2,2048]{1,0:T(2,128)(2,1)S(1)} collective-permute-done((bf16[2,2048]{1,0:T(2,128)(2,1)S(1)}, bf16[2,2048]{1,0:T(2,128)(2,1)S(1)}, u32[]{:S(2)}, u32[]{:S(2)}) %collective-permute-start) | collective-permute-done | bytes 8224 | tf_op jit(solution)/shard_map/while/body/eval_jaxpr/ppermute | solution.py:14
  771.2 8.6 %all-to-all-done = bf16[16,2,2048]{2,1,0:T(2,128)(2,1)S(1)} async-done(((bf16[16,2,2048]{2,1,0:T(2,128)(2,1)}), bf16[16,2,2048]{2,1,0:T(2,128)(2,1)S(1)}, u32[]{:S(2)}, u32[]{:S(2)}) %all-to-all-start) | async-done | bytes 131104 | tf_op jit(solution)/shard_map/while/body/eval_jaxpr/all_to_all | solution.py:74
  779.8 6.4 conditional.2
  787.5 7.5 collective-permute-done
  800.1 8.6 %all-to-all-done = bf16[16,2,2048]{2,1,0:T(2,128)(2,1)S(1)} async-done(((bf16[16,2,2048]{2,1,0:T(2,128)(2,1)}), bf16[16,2,2048]{2,1,0:T(2,128)(2,1)S(1)}, u32[]{:S(2)}, u32[]{:S(2)}) %all-to-all-start) | async-done | bytes 131104 | tf_op jit(solution)/shard_map/while/body/eval_jaxpr/all_to_all | solution.py:74
  808.7 6.4 conditional.2
  816.4 7.5 collective-permute-done
  829.0 8.6 %all-to-all-done = bf16[16,2,2048]{2,1,0:T(2,128)(2,1)S(1)} async-done(((bf16[16,2,2048]{2,1,0:T(2,128)(2,1)}), bf16[16,2,2048]{2,1,0:T(2,128)(2,1)S(1)}, u32[]{:S(2)}, u32[]{:S(2)}) %all-to-all-start) | async-done | bytes 131104 | tf_op jit(solution)/shard_map/while/body/eval_jaxpr/all_to_all | solution.py:74
  837.6 6.4 conditional.2
  (274 shorter events, 277.0 us)
Async XLA Ops:
  1.5 15.9 %all-to-all-start = ((bf16[16,2,2048]{2,1,0:T(2,128)(2,1)}), bf16[16,2,2048]{2,1,0:T(2,128)(2,1)S(1)}, u32[]{:S(2)}, u32[]{:S(2)}) async-start(bf16[16,2,2048]{2,1,0:T(2,128)(2,1)} %stack.7), calls=%async_computation | async-start | bytes 262144 | tf_op jit(solution)/shard_map/while/body/eval_jaxpr/all_to_all | solution.py:74
  17.4 5.5 collective-permute-start
  24.4 12.1 %all-to-all-start = ((bf16[16,2,2048]{2,1,0:T(2,128)(2,1)}), bf16[16,2,2048]{2,1,0:T(2,128)(2,1)S(1)}, u32[]{:S(2)}, u32[]{:S(2)}) async-start(bf16[16,2,2048]{2,1,0:T(2,128)(2,1)} %stack.7), calls=%async_computation | async-start | bytes 262144 | tf_op jit(solution)/shard_map/while/body/eval_jaxpr/all_to_all | solution.py:74
  43.7 12.1 %all-to-all-start = ((bf16[16,2,2048]{2,1,0:T(2,128)(2,1)}), bf16[16,2,2048]{2,1,0:T(2,128)(2,1)S(1)}, u32[]{:S(2)}, u32[]{:S(2)}) async-start(bf16[16,2,2048]{2,1,0:T(2,128)(2,1)} %stack.7), calls=%async_computation | async-start | bytes 262144 | tf_op jit(solution)/shard_map/while/body/eval_jaxpr/all_to_all | solution.py:74
  62.9 12.1 %all-to-all-start = ((bf16[16,2,2048]{2,1,0:T(2,128)(2,1)}), bf16[16,2,2048]{2,1,0:T(2,128)(2,1)S(1)}, u32[]{:S(2)}, u32[]{:S(2)}) async-start(bf16[16,2,2048]{2,1,0:T(2,128)(2,1)} %stack.7), calls=%async_computation | async-start | bytes 262144 | tf_op jit(solution)/shard_map/while/body/eval_jaxpr/all_to_all | solution.py:74
  82.1 12.1 %all-to-all-start = ((bf16[16,2,2048]{2,1,0:T(2,128)(2,1)}), bf16[16,2,2048]{2,1,0:T(2,128)(2,1)S(1)}, u32[]{:S(2)}, u32[]{:S(2)}) async-start(bf16[16,2,2048]{2,1,0:T(2,128)(2,1)} %stack.7), calls=%async_computation | async-start | bytes 262144 | tf_op jit(solution)/shard_map/while/body/eval_jaxpr/all_to_all | solution.py:74
  94.2 5.6 collective-permute-start
  101.4 12.1 %all-to-all-start = ((bf16[16,2,2048]{2,1,0:T(2,128)(2,1)}), bf16[16,2,2048]{2,1,0:T(2,128)(2,1)S(1)}, u32[]{:S(2)}, u32[]{:S(2)}) async-start(bf16[16,2,2048]{2,1,0:T(2,128)(2,1)} %stack.7), calls=%async_computation | async-start | bytes 262144 | tf_op jit(solution)/shard_map/while/body/eval_jaxpr/all_to_all | solution.py:74
  113.5 7.7 collective-permute-start
  122.7 12.1 %all-to-all-start = ((bf16[16,2,2048]{2,1,0:T(2,128)(2,1)}), bf16[16,2,2048]{2,1,0:T(2,128)(2,1)S(1)}, u32[]{:S(2)}, u32[]{:S(2)}) async-start(bf16[16,2,2048]{2,1,0:T(2,128)(2,1)} %stack.7), calls=%async_computation | async-start | bytes 262144 | tf_op jit(solution)/shard_map/while/body/eval_jaxpr/all_to_all | solution.py:74
  134.8 7.7 collective-permute-start
  144.0 12.1 %all-to-all-start = ((bf16[16,2,2048]{2,1,0:T(2,128)(2,1)}), bf16[16,2,2048]{2,1,0:T(2,128)(2,1)S(1)}, u32[]{:S(2)}, u32[]{:S(2)}) async-start(bf16[16,2,2048]{2,1,0:T(2,128)(2,1)} %stack.7), calls=%async_computation | async-start | bytes 262144 | tf_op jit(solution)/shard_map/while/body/eval_jaxpr/all_to_all | solution.py:74
  156.1 7.7 collective-permute-start
  165.3 12.1 %all-to-all-start = ((bf16[16,2,2048]{2,1,0:T(2,128)(2,1)}), bf16[16,2,2048]{2,1,0:T(2,128)(2,1)S(1)}, u32[]{:S(2)}, u32[]{:S(2)}) async-start(bf16[16,2,2048]{2,1,0:T(2,128)(2,1)} %stack.7), calls=%async_computation | async-start | bytes 262144 | tf_op jit(solution)/shard_map/while/body/eval_jaxpr/all_to_all | solution.py:74
  177.5 7.7 collective-permute-start
  186.6 12.1 %all-to-all-start = ((bf16[16,2,2048]{2,1,0:T(2,128)(2,1)}), bf16[16,2,2048]{2,1,0:T(2,128)(2,1)S(1)}, u32[]{:S(2)}, u32[]{:S(2)}) async-start(bf16[16,2,2048]{2,1,0:T(2,128)(2,1)} %stack.7), calls=%async_computation | async-start | bytes 262144 | tf_op jit(solution)/shard_map/while/body/eval_jaxpr/all_to_all | solution.py:74
  198.8 7.7 collective-permute-start
  208.0 12.1 %all-to-all-start = ((bf16[16,2,2048]{2,1,0:T(2,128)(2,1)}), bf16[16,2,2048]{2,1,0:T(2,128)(2,1)S(1)}, u32[]{:S(2)}, u32[]{:S(2)}) async-start(bf16[16,2,2048]{2,1,0:T(2,128)(2,1)} %stack.7), calls=%async_computation | async-start | bytes 262144 | tf_op jit(solution)/shard_map/while/body/eval_jaxpr/all_to_all | solution.py:74
  220.1 7.7 collective-permute-start
  229.3 12.1 %all-to-all-start = ((bf16[16,2,2048]{2,1,0:T(2,128)(2,1)}), bf16[16,2,2048]{2,1,0:T(2,128)(2,1)S(1)}, u32[]{:S(2)}, u32[]{:S(2)}) async-start(bf16[16,2,2048]{2,1,0:T(2,128)(2,1)} %stack.7), calls=%async_computation | async-start | bytes 262144 | tf_op jit(solution)/shard_map/while/body/eval_jaxpr/all_to_all | solution.py:74
  241.4 7.7 collective-permute-start
  250.6 12.1 %all-to-all-start = ((bf16[16,2,2048]{2,1,0:T(2,128)(2,1)}), bf16[16,2,2048]{2,1,0:T(2,128)(2,1)S(1)}, u32[]{:S(2)}, u32[]{:S(2)}) async-start(bf16[16,2,2048]{2,1,0:T(2,128)(2,1)} %stack.7), calls=%async_computation | async-start | bytes 262144 | tf_op jit(solution)/shard_map/while/body/eval_jaxpr/all_to_all | solution.py:74
  262.7 7.7 collective-permute-start
  271.9 12.1 %all-to-all-start = ((bf16[16,2,2048]{2,1,0:T(2,128)(2,1)}), bf16[16,2,2048]{2,1,0:T(2,128)(2,1)S(1)}, u32[]{:S(2)}, u32[]{:S(2)}) async-start(bf16[16,2,2048]{2,1,0:T(2,128)(2,1)} %stack.7), calls=%async_computation | async-start | bytes 262144 | tf_op jit(solution)/shard_map/while/body/eval_jaxpr/all_to_all | solution.py:74
  284.1 7.7 collective-permute-start
  293.2 12.1 %all-to-all-start = ((bf16[16,2,2048]{2,1,0:T(2,128)(2,1)}), bf16[16,2,2048]{2,1,0:T(2,128)(2,1)S(1)}, u32[]{:S(2)}, u32[]{:S(2)}) async-start(bf16[16,2,2048]{2,1,0:T(2,128)(2,1)} %stack.7), calls=%async_computation | async-start | bytes 262144 | tf_op jit(solution)/shard_map/while/body/eval_jaxpr/all_to_all | solution.py:74
  305.4 7.7 collective-permute-start
  314.5 12.1 %all-to-all-start = ((bf16[16,2,2048]{2,1,0:T(2,128)(2,1)}), bf16[16,2,2048]{2,1,0:T(2,128)(2,1)S(1)}, u32[]{:S(2)}, u32[]{:S(2)}) async-start(bf16[16,2,2048]{2,1,0:T(2,128)(2,1)} %stack.7), calls=%async_computation | async-start | bytes 262144 | tf_op jit(solution)/shard_map/while/body/eval_jaxpr/all_to_all | solution.py:74
  326.7 7.7 collective-permute-start
  335.9 12.1 %all-to-all-start = ((bf16[16,2,2048]{2,1,0:T(2,128)(2,1)}), bf16[16,2,2048]{2,1,0:T(2,128)(2,1)S(1)}, u32[]{:S(2)}, u32[]{:S(2)}) async-start(bf16[16,2,2048]{2,1,0:T(2,128)(2,1)} %stack.7), calls=%async_computation | async-start | bytes 262144 | tf_op jit(solution)/shard_map/while/body/eval_jaxpr/all_to_all | solution.py:74
  348.0 7.7 collective-permute-start
  357.2 12.1 %all-to-all-start = ((bf16[16,2,2048]{2,1,0:T(2,128)(2,1)}), bf16[16,2,2048]{2,1,0:T(2,128)(2,1)S(1)}, u32[]{:S(2)}, u32[]{:S(2)}) async-start(bf16[16,2,2048]{2,1,0:T(2,128)(2,1)} %stack.7), calls=%async_computation | async-start | bytes 262144 | tf_op jit(solution)/shard_map/while/body/eval_jaxpr/all_to_all | solution.py:74
  369.3 7.7 collective-permute-start
  378.5 12.1 %all-to-all-start = ((bf16[16,2,2048]{2,1,0:T(2,128)(2,1)}), bf16[16,2,2048]{2,1,0:T(2,128)(2,1)S(1)}, u32[]{:S(2)}, u32[]{:S(2)}) async-start(bf16[16,2,2048]{2,1,0:T(2,128)(2,1)} %stack.7), calls=%async_computation | async-start | bytes 262144 | tf_op jit(solution)/shard_map/while/body/eval_jaxpr/all_to_all | solution.py:74
  390.7 7.7 collective-permute-start
  399.8 12.1 %all-to-all-start = ((bf16[16,2,2048]{2,1,0:T(2,128)(2,1)}), bf16[16,2,2048]{2,1,0:T(2,128)(2,1)S(1)}, u32[]{:S(2)}, u32[]{:S(2)}) async-start(bf16[16,2,2048]{2,1,0:T(2,128)(2,1)} %stack.7), calls=%async_computation | async-start | bytes 262144 | tf_op jit(solution)/shard_map/while/body/eval_jaxpr/all_to_all | solution.py:74
  412.0 7.7 collective-permute-start
  421.1 12.1 %all-to-all-start = ((bf16[16,2,2048]{2,1,0:T(2,128)(2,1)}), bf16[16,2,2048]{2,1,0:T(2,128)(2,1)S(1)}, u32[]{:S(2)}, u32[]{:S(2)}) async-start(bf16[16,2,2048]{2,1,0:T(2,128)(2,1)} %stack.7), calls=%async_computation | async-start | bytes 262144 | tf_op jit(solution)/shard_map/while/body/eval_jaxpr/all_to_all | solution.py:74
  433.3 7.7 collective-permute-start
  442.5 12.1 %all-to-all-start = ((bf16[16,2,2048]{2,1,0:T(2,128)(2,1)}), bf16[16,2,2048]{2,1,0:T(2,128)(2,1)S(1)}, u32[]{:S(2)}, u32[]{:S(2)}) async-start(bf16[16,2,2048]{2,1,0:T(2,128)(2,1)} %stack.7), calls=%async_computation | async-start | bytes 262144 | tf_op jit(solution)/shard_map/while/body/eval_jaxpr/all_to_all | solution.py:74
  454.6 7.7 collective-permute-start
  463.8 12.1 %all-to-all-start = ((bf16[16,2,2048]{2,1,0:T(2,128)(2,1)}), bf16[16,2,2048]{2,1,0:T(2,128)(2,1)S(1)}, u32[]{:S(2)}, u32[]{:S(2)}) async-start(bf16[16,2,2048]{2,1,0:T(2,128)(2,1)} %stack.7), calls=%async_computation | async-start | bytes 262144 | tf_op jit(solution)/shard_map/while/body/eval_jaxpr/all_to_all | solution.py:74
  475.9 7.7 collective-permute-start
  485.1 12.1 %all-to-all-start = ((bf16[16,2,2048]{2,1,0:T(2,128)(2,1)}), bf16[16,2,2048]{2,1,0:T(2,128)(2,1)S(1)}, u32[]{:S(2)}, u32[]{:S(2)}) async-start(bf16[16,2,2048]{2,1,0:T(2,128)(2,1)} %stack.7), calls=%async_computation | async-start | bytes 262144 | tf_op jit(solution)/shard_map/while/body/eval_jaxpr/all_to_all | solution.py:74
  497.2 7.7 collective-permute-start
  506.4 12.1 %all-to-all-start = ((bf16[16,2,2048]{2,1,0:T(2,128)(2,1)}), bf16[16,2,2048]{2,1,0:T(2,128)(2,1)S(1)}, u32[]{:S(2)}, u32[]{:S(2)}) async-start(bf16[16,2,2048]{2,1,0:T(2,128)(2,1)} %stack.7), calls=%async_computation | async-start | bytes 262144 | tf_op jit(solution)/shard_map/while/body/eval_jaxpr/all_to_all | solution.py:74
  518.6 7.7 collective-permute-start
  527.7 12.1 %all-to-all-start = ((bf16[16,2,2048]{2,1,0:T(2,128)(2,1)}), bf16[16,2,2048]{2,1,0:T(2,128)(2,1)S(1)}, u32[]{:S(2)}, u32[]{:S(2)}) async-start(bf16[16,2,2048]{2,1,0:T(2,128)(2,1)} %stack.7), calls=%async_computation | async-start | bytes 262144 | tf_op jit(solution)/shard_map/while/body/eval_jaxpr/all_to_all | solution.py:74
  539.9 7.7 collective-permute-start
  549.1 12.1 %all-to-all-start = ((bf16[16,2,2048]{2,1,0:T(2,128)(2,1)}), bf16[16,2,2048]{2,1,0:T(2,128)(2,1)S(1)}, u32[]{:S(2)}, u32[]{:S(2)}) async-start(bf16[16,2,2048]{2,1,0:T(2,128)(2,1)} %stack.7), calls=%async_computation | async-start | bytes 262144 | tf_op jit(solution)/shard_map/while/body/eval_jaxpr/all_to_all | solution.py:74
  561.2 7.7 collective-permute-start
  570.4 12.1 %all-to-all-start = ((bf16[16,2,2048]{2,1,0:T(2,128)(2,1)}), bf16[16,2,2048]{2,1,0:T(2,128)(2,1)S(1)}, u32[]{:S(2)}, u32[]{:S(2)}) async-start(bf16[16,2,2048]{2,1,0:T(2,128)(2,1)} %stack.7), calls=%async_computation | async-start | bytes 262144 | tf_op jit(solution)/shard_map/while/body/eval_jaxpr/all_to_all | solution.py:74
  582.5 7.7 collective-permute-start
  591.7 12.1 %all-to-all-start = ((bf16[16,2,2048]{2,1,0:T(2,128)(2,1)}), bf16[16,2,2048]{2,1,0:T(2,128)(2,1)S(1)}, u32[]{:S(2)}, u32[]{:S(2)}) async-start(bf16[16,2,2048]{2,1,0:T(2,128)(2,1)} %stack.7), calls=%async_computation | async-start | bytes 262144 | tf_op jit(solution)/shard_map/while/body/eval_jaxpr/all_to_all | solution.py:74
  603.8 7.7 collective-permute-start
  613.0 12.1 %all-to-all-start = ((bf16[16,2,2048]{2,1,0:T(2,128)(2,1)}), bf16[16,2,2048]{2,1,0:T(2,128)(2,1)S(1)}, u32[]{:S(2)}, u32[]{:S(2)}) async-start(bf16[16,2,2048]{2,1,0:T(2,128)(2,1)} %stack.7), calls=%async_computation | async-start | bytes 262144 | tf_op jit(solution)/shard_map/while/body/eval_jaxpr/all_to_all | solution.py:74
  625.2 7.7 collective-permute-start
  634.3 12.1 %all-to-all-start = ((bf16[16,2,2048]{2,1,0:T(2,128)(2,1)}), bf16[16,2,2048]{2,1,0:T(2,128)(2,1)S(1)}, u32[]{:S(2)}, u32[]{:S(2)}) async-start(bf16[16,2,2048]{2,1,0:T(2,128)(2,1)} %stack.7), calls=%async_computation | async-start | bytes 262144 | tf_op jit(solution)/shard_map/while/body/eval_jaxpr/all_to_all | solution.py:74
  646.5 119.7 %collective-permute-start = (bf16[2,2048]{1,0:T(2,128)(2,1)S(1)}, bf16[2,2048]{1,0:T(2,128)(2,1)S(1)}, u32[]{:S(2)}, u32[]{:S(2)}) collective-permute-start(bf16[2,2048]{1,0:T(2,128)(2,1)S(1)} %get-tuple-element.355), channel_id=1, source_target_pairs={{0,16},{16,32},{32,48},{48,64},{64,80},{80,96},{96,112},{112,128},... | collective-permute-start | bytes 24584 | tf_op jit(solution)/shard_map/while/body/eval_jaxpr/ppermute | solution.py:14
  767.7 12.1 %all-to-all-start = ((bf16[16,2,2048]{2,1,0:T(2,128)(2,1)}), bf16[16,2,2048]{2,1,0:T(2,128)(2,1)S(1)}, u32[]{:S(2)}, u32[]{:S(2)}) async-start(bf16[16,2,2048]{2,1,0:T(2,128)(2,1)} %stack.7), calls=%async_computation | async-start | bytes 262144 | tf_op jit(solution)/shard_map/while/body/eval_jaxpr/all_to_all | solution.py:74
  786.2 8.9 %collective-permute-start = (bf16[2,2048]{1,0:T(2,128)(2,1)S(1)}, bf16[2,2048]{1,0:T(2,128)(2,1)S(1)}, u32[]{:S(2)}, u32[]{:S(2)}) collective-permute-start(bf16[2,2048]{1,0:T(2,128)(2,1)S(1)} %get-tuple-element.355), channel_id=1, source_target_pairs={{0,16},{16,32},{32,48},{48,64},{64,80},{80,96},{96,112},{112,128},... | collective-permute-start | bytes 24584 | tf_op jit(solution)/shard_map/while/body/eval_jaxpr/ppermute | solution.py:14
  796.6 12.1 %all-to-all-start = ((bf16[16,2,2048]{2,1,0:T(2,128)(2,1)}), bf16[16,2,2048]{2,1,0:T(2,128)(2,1)S(1)}, u32[]{:S(2)}, u32[]{:S(2)}) async-start(bf16[16,2,2048]{2,1,0:T(2,128)(2,1)} %stack.7), calls=%async_computation | async-start | bytes 262144 | tf_op jit(solution)/shard_map/while/body/eval_jaxpr/all_to_all | solution.py:74
  815.1 8.9 %collective-permute-start = (bf16[2,2048]{1,0:T(2,128)(2,1)S(1)}, bf16[2,2048]{1,0:T(2,128)(2,1)S(1)}, u32[]{:S(2)}, u32[]{:S(2)}) collective-permute-start(bf16[2,2048]{1,0:T(2,128)(2,1)S(1)} %get-tuple-element.355), channel_id=1, source_target_pairs={{0,16},{16,32},{32,48},{48,64},{64,80},{80,96},{96,112},{112,128},... | collective-permute-start | bytes 24584 | tf_op jit(solution)/shard_map/while/body/eval_jaxpr/ppermute | solution.py:14
  825.5 12.1 %all-to-all-start = ((bf16[16,2,2048]{2,1,0:T(2,128)(2,1)}), bf16[16,2,2048]{2,1,0:T(2,128)(2,1)S(1)}, u32[]{:S(2)}, u32[]{:S(2)}) async-start(bf16[16,2,2048]{2,1,0:T(2,128)(2,1)} %stack.7), calls=%async_computation | async-start | bytes 262144 | tf_op jit(solution)/shard_map/while/body/eval_jaxpr/all_to_all | solution.py:74
  (8 other events, 41.4 us)
